TPU v7x, 512 devices: a whole 4x8x8 slice. The times are simulated.
512 devices in a mesh: seq: 128 (over x, z_hi, y, core), tp: 4 (over z_lo).
Axes of the slice: x: 4, y: 8, z: 8 (z_hi: 2, z_lo: 4; z = z_hi * 4 + z_lo), core: 2. Of those that a mesh axis runs over, the one named last changes fastest.
Arguments:
- queries: bfloat16 [16384, 4096], P('seq', 'tp'), may hold values from -6 to 6
- suffix_entries: bfloat16 [16384, 4096], P('seq', 'tp'), may hold values from -6 to 6
- prefix_cache: bfloat16 [2048, 4096], P(('seq', 'tp')), may hold values from -6 to 6
- block_prefix: int32 [512], replicated, may hold values from 0 to 1, as said below
- request_lengths: int32 [512], P('seq'), may hold values from 0 to 128, as said below
- request_prefix: int32 [512], P('seq'), may hold values from 0 to 1
Outputs:
- attended: bfloat16 [16384, 4096], P('seq', 'tp')
Inputs may be any that keep to these rules, and one draw needn't show every extreme that they name: `request_lengths`: the lengths of one index of seq's requests sum to at most 128; at some index they sum to exactly 128, and there one request alone takes all 128 slots. `block_prefix`: exactly half of the blocks belong to each prefix.
All inputs are finite; a program needn't handle non-finite values.
Results may differ from a plain program's by a relative error of at most 0.0049.
Values may be sent and summed in bfloat16 or wider, within the bound.
No kernel may reach another device: no remote copies, remote signals or barrier semaphores. Data moves between devices by JAX's collectives and lax.ppermute only.
A program may use at most 64 MiB of HBM per device.

v0:
```python
import math
import jax
import jax.numpy as jnp
from jax import lax
from jax.sharding import PartitionSpec as P

HEADS = 16
HEAD = 128
masked_score = -1e30
section_rows = 512


def token_layout(lengths, prefixes, slots):
    cumulative = jnp.cumsum(lengths)
    slot_ids = jnp.arange(slots, dtype=jnp.int32)
    request_ids = jnp.sum((slot_ids[:, None] >= cumulative[None, :]).astype(jnp.int32), axis=1)
    live_slots = slot_ids < cumulative[-1]
    onehot = request_ids[:, None] == jnp.arange(lengths.shape[0], dtype=jnp.int32)[None, :]
    token_group = jnp.sum(jnp.where(onehot, prefixes[None, :], 0), axis=1)
    return (slot_ids, request_ids, live_slots, token_group)


def attend(running, query_rows, key_rows, value_rows, allowed):
    old_max, old_total, old_sum = running
    scores = jnp.einsum("thed,rhd->ther", query_rows, key_rows, preferred_element_type=jnp.float32)
    scores = scores * (1.0 / math.sqrt(query_rows.shape[-1]))
    allowed_grid = allowed[:, None, None, :]
    scores = jnp.where(allowed_grid, scores, masked_score)
    new_max = jnp.maximum(old_max, jnp.max(scores, axis=-1))
    rescale = jnp.exp(old_max - new_max)
    weights = jnp.where(allowed_grid, jnp.exp(scores - new_max[..., None]), 0.0)
    new_total = old_total * rescale + jnp.sum(weights, axis=-1)
    products = jnp.einsum(
        "ther,rhd->thed",
        weights.astype(jnp.bfloat16),
        value_rows,
        preferred_element_type=jnp.float32,
    )
    new_sum = old_sum * rescale[..., None] + products
    return (new_max, new_total, new_sum)


def owner_lookup(block_ids, block_prefix):
    match = block_ids[:, None] == jnp.arange(block_prefix.shape[0], dtype=jnp.int32)[None, :]
    return jnp.sum(jnp.where(match, block_prefix[None, :], 0), axis=1)


def empty_state(token_rows, head_count):
    return (
        jnp.full((token_rows, head_count, 2), masked_score, jnp.float32),
        jnp.zeros((token_rows, head_count, 2), jnp.float32),
        jnp.zeros((token_rows, head_count, 2, HEAD), jnp.float32),
    )


def sweep(running, query_rows, rows, head_count, block_of, block_prefix, token_group, live_slots):
    total_rows = rows.shape[0]
    for offset in range(0, total_rows, section_rows):
        row_count = min(section_rows, total_rows - offset)
        section = rows[offset : offset + row_count].reshape(row_count, head_count, 2, HEAD)
        positions = offset + jnp.arange(row_count, dtype=jnp.int32)
        owners = owner_lookup(block_of(positions), block_prefix)
        allowed = (token_group[:, None] == owners[None, :]) & live_slots[:, None]
        running = attend(running, query_rows, section[:, :, 0], section[:, :, 1], allowed)
    return running


def per_device(
    queries, suffix_entries, prefix_cache, block_prefix, request_lengths, request_prefix
):
    tensor_count = lax.axis_size("tp")
    seq_count = lax.axis_size("seq")
    local_heads = HEADS // tensor_count
    token_rows = queries.shape[0]
    block_rows = prefix_cache.shape[0]
    slot_ids, request_ids, live_slots, token_group = token_layout(
        request_lengths, request_prefix, token_rows
    )
    own_query = queries.reshape(token_rows, local_heads, 2, HEAD)
    own_entries = suffix_entries.reshape(token_rows, local_heads, 2, HEAD)
    gathered = lax.all_gather(prefix_cache, "seq", axis=0, tiled=True)
    cached = lax.all_to_all(gathered, "tp", split_axis=1, concat_axis=0, tiled=True)
    span = seq_count * block_rows

    def block_of(positions):
        return positions % span // block_rows * tensor_count + positions // span

    running = sweep(
        empty_state(token_rows, local_heads),
        own_query,
        cached,
        local_heads,
        block_of,
        block_prefix,
        token_group,
        live_slots,
    )
    suffix_allowed = (
        (request_ids[:, None] == request_ids[None, :])
        & (slot_ids[None, :] <= slot_ids[:, None])
        & live_slots[:, None]
    )
    running = attend(running, own_query, own_entries[:, :, 0], own_entries[:, :, 1], suffix_allowed)
    final_max, final_total, final_sum = running
    live_grid = live_slots[:, None, None]
    safe_total = jnp.where(live_grid, final_total, 1.0)
    result = jnp.where(live_grid[..., None], final_sum / safe_total[..., None], 0.0)
    return result.astype(jnp.bfloat16).reshape(token_rows, local_heads * 2 * HEAD)


def solution(mesh):
    in_specs = (P("seq", "tp"), P("seq", "tp"), P(("seq", "tp"), None), P(), P("seq"), P("seq"))
    out_specs = P("seq", "tp")
    return jax.shard_map(
        per_device, mesh=mesh, in_specs=in_specs, out_specs=out_specs, check_vma=False
    )
```

profile of v0, /device:TPU:1, one launch (start us, length us, event | category | flops | bytes accessed | tf_op | source)
XLA Modules:
  0.0 292.7 jit_solution(12591821938182171553)
XLA Ops:
  6.5 0.7 all-gather.3.cloned.1.call-update
  7.3 150.3 %all-gather.3.cloned.1.call-done = bf16[128,4,4096]{2,1,0:T(4,128)(2,1)} async-done(((bf16[1,4,4096]{2,1,0:T(4,128)(2,1)}), bf16[128,4,4096]{2,1,0:T(4,128)(2,1)}) %all-gather.3.cloned.1.call-update) | async-done | bytes 4194320 | tf_op jit(solution)/shard_map/all_gather | solution.py:81
  157.6 7.9 %all_to_all.12 = bf16[512,4,1024]{2,1,0:T(4,128)(2,1)} reshape(bf16[128,4,4096]{2,1,0:T(4,128)(2,1)} %all-gather.3.cloned.1.call-done) | data formatting | bytes 8388608 | tf_op jit(solution)/shard_map/all_to_all | solution.py:82
  165.4 5.5 %copy.96 = bf16[512,4,1024]{2,0,1:T(8,128)(2,1)} copy(bf16[512,4,1024]{2,1,0:T(4,128)(2,1)} %all_to_all.12) | data formatting | bytes 8388608 | tf_op jit(solution)/shard_map/all_to_all | solution.py:82
  171.0 5.0 %all-to-all-start = ((bf16[512,4,1024]{2,0,1:T(8,128)(2,1)}), bf16[512,4,1024]{2,0,1:T(8,128)(2,1)}, u32[]{:S(2)}, u32[]{:S(2)}) async-start(bf16[512,4,1024]{2,0,1:T(8,128)(2,1)} %copy.96), calls=%async_computation | async-start | bytes 8388608 | tf_op jit(solution)/shard_map/all_to_all | solution.py:82
  176.2 0.6 slice.50
  177.1 0.7 iota_compare_fusion.7
  178.0 0.9 select_reduce_fusion
  179.6 89.3 %all-to-all-done = bf16[512,4,1024]{2,0,1:T(8,128)(2,1)} async-done(((bf16[512,4,1024]{2,0,1:T(8,128)(2,1)}), bf16[512,4,1024]{2,0,1:T(8,128)(2,1)}, u32[]{:S(2)}, u32[]{:S(2)}) %all-to-all-start) | async-done | bytes 4194336 | tf_op jit(solution)/shard_map/all_to_all | solution.py:82
  269.0 6.2 %copy.97 = bf16[512,4,1024]{0,2,1:T(8,128)(2,1)} copy(bf16[512,4,1024]{2,0,1:T(8,128)(2,1)} %all-to-all-done) | data formatting | bytes 8388608 | tf_op jit(solution)/shard_map/all_to_all | solution.py:82
  275.2 2.4 fusion.108
  277.6 0.5 fusion.1
  278.2 0.5 fusion.2
  278.7 0.5 fusion.3
  279.3 0.5 fusion
  279.8 0.5 fusion.4
  280.5 0.5 fusion.10
  281.0 0.5 fusion.8
  281.5 0.5 fusion.6
  282.1 0.7 fusion.19
  282.8 0.7 fusion.17
  283.4 0.7 fusion.15
  284.1 0.7 fusion.13
  285.1 0.9 copy.119
  (25 shorter events, 1.9 us)
Async XLA Ops:
  6.5 151.0 %all-gather.3.cloned.1.call-start = ((), (), s32[]{:S(2)}) async-start(), calls=%async_computation.1 | async-start | bytes 4227072 | tf_op jit(solution)/shard_map/all_gather | solution.py:81
  170.9 5.0 %copy-start.3 = (s32[4]{0:T(128)S(1)}, s32[4]{0:T(128)}, u32[]{:S(2)}) copy-start(s32[4]{0:T(128)} %param.10) | copy-start | bytes 52
  170.9 5.8 %copy-start = (bf16[128,1024]{1,0:T(8,128)(2,1)S(1)}, bf16[128,1024]{1,0:T(8,128)(2,1)}, u32[]{:S(2)}) copy-start(bf16[128,1024]{1,0:T(8,128)(2,1)} %param.6) | copy-start | bytes 786436
  170.9 6.0 %copy-start.1 = (bf16[128,1024]{1,0:T(8,128)(2,1)S(1)}, bf16[128,1024]{1,0:T(8,128)(2,1)}, u32[]{:S(2)}) copy-start(bf16[128,1024]{1,0:T(8,128)(2,1)} %param.7) | copy-start | bytes 786436
  170.9 6.9 %copy-start.4 = (s32[4]{0:T(128)S(1)}, s32[4]{0:T(128)}, u32[]{:S(2)}) copy-start(s32[4]{0:T(128)} %param.11) | copy-start | bytes 52
  171.0 7.0 %copy-start.2 = (s32[512]{0:T(512)S(1)}, s32[512]{0:T(512)}, u32[]{:S(2)}) copy-start(s32[512]{0:T(512)} %param.9) | copy-start | bytes 6148
  171.0 98.0 %all-to-all-start = ((bf16[512,4,1024]{2,0,1:T(8,128)(2,1)}), bf16[512,4,1024]{2,0,1:T(8,128)(2,1)}, u32[]{:S(2)}, u32[]{:S(2)}) async-start(bf16[512,4,1024]{2,0,1:T(8,128)(2,1)} %copy.96), calls=%async_computation | async-start | bytes 8388608 | tf_op jit(solution)/shard_map/all_to_all | solution.py:82
Sparse Core Ops, SparseCore 0:
  11.9 145.6 all-gather.2
where the time goes:
time: 293 us
  waiting for transfers between devices  240 us (82%)
  local copies, waits for them, and re-layouts  23.8 us (8%)
  between operations  13.6 us (5%)
  matrix products  5.38 us (2%)
  starting transfers between devices  5 us (2%)
  other arithmetic  4.64 us (2%)
    all_gather x1, waiting for transfers between devices, per_device(): gathered = lax.all_gather(prefix_cache, 'seq', axis=0, tiled=True)  150 us
    all_to_all x1, waiting for transfers between devices, per_device(): lax.all_to_all(gathered, 'tp', split_axis=1, concat_axis=0, tiled=True)  89.3 us
    all_to_all x3, local copies, waits for them, and re-layouts, per_device(): lax.all_to_all(gathered, 'tp', split_axis=1, concat_axis=0, tiled=True)  19.6 us
  transfers between devices with their start and end apart: 2, of which 2 were waited for; matrix products, arithmetic and copies ran while one was open for 1% of the time, Pallas kernels for 0%

commit v1 on v0

--- a/solution.py
+++ b/solution.py
@@ -79,7 +79,10 @@
     own_query = queries.reshape(token_rows, local_heads, 2, HEAD)
     own_entries = suffix_entries.reshape(token_rows, local_heads, 2, HEAD)
     gathered = lax.all_gather(prefix_cache, "seq", axis=0, tiled=True)
-    cached = lax.all_to_all(gathered, "tp", split_axis=1, concat_axis=0, tiled=True)
+    cached = jnp.concatenate(
+        lax.all_to_all(jnp.stack(jnp.split(gathered, lax.axis_size("tp"), axis=1)), "tp", 0, 0),
+        axis=0,
+    )
     span = seq_count * block_rows
 
     def block_of(positions):

time: 293 us -> 294 us (level)
  local copies, waits for them, and re-layouts: 23.8 us -> 20.8 us
    all_to_all x3 -> x0, local copies, waits for them, and re-layouts: 19.6 us -> none  [per_device(): lax.all_to_all(gathered, 'tp', split_axis=1, concat_axis=0, tiled=True)]
    unnamed x11 -> x32, local copies, waits for them, and re-layouts: 0.19 us -> 8.06 us
    slice x1 -> x5, local copies, waits for them, and re-layouts: 2.44 us -> 8.56 us  [sweep(): rows[offset:offset + row_count].reshape(row_count, head_count, 2, HEAD)]
  transfers between devices with their start and end apart: 2 -> 2, of which waited for: 2 -> 2; matrix products, arithmetic and copies ran while one was open for 1% -> 2% of each run, Pallas kernels for 0% -> 0%
where the time goes in v1:
time: 294 us; the launch traced here: 293 us
  waiting for transfers between devices  238 us (81%)
  local copies, waits for them, and re-layouts  20.8 us (7%)
  between operations  13.7 us (5%)
  matrix products  7.79 us (3%)
  other arithmetic  7.44 us (3%)
  starting transfers between devices  5 us (2%)
    all_gather x1, waiting for transfers between devices, per_device(): gathered = lax.all_gather(prefix_cache, 'seq', axis=0, tiled=True)  150 us
    all_to_all x1, waiting for transfers between devices, per_device(): lax.all_to_all(jnp.stack(jnp.split(gathered, lax.axis_size('tp'), axis=1)...  87.4 us
    slice x5, local copies, waits for them, and re-layouts, sweep(): rows[offset:offset + row_count].reshape(row_count, head_count, 2, HEAD)  8.56 us
    unnamed x32, local copies, waits for them, and re-layouts  8.06 us
  transfers between devices with their start and end apart: 2, of which 2 were waited for; matrix products, arithmetic and copies ran while one was open for 2% of the time, Pallas kernels for 0%

profile of v1, /device:TPU:1, one launch (start us, length us, event | category | flops | bytes accessed | tf_op | source)
XLA Modules:
  0.0 293.1 jit_solution(7256748601088628219)
XLA Ops:
  6.5 0.7 all-gather.3.cloned.1.call-update
  7.3 150.3 %all-gather.3.cloned.1.call-done = bf16[128,4,4096]{2,1,0:T(4,128)(2,1)} async-done(((bf16[1,4,4096]{2,1,0:T(4,128)(2,1)}), bf16[128,4,4096]{2,1,0:T(4,128)(2,1)}) %all-gather.3.cloned.1.call-update) | async-done | bytes 4194320 | tf_op jit(solution)/shard_map/all_gather | solution.py:81
  157.6 6.9 %reshape.525 = bf16[512,4096]{1,0:T(8,128)(2,1)} reshape(bf16[128,4,4096]{2,1,0:T(4,128)(2,1)} %all-gather.3.cloned.1.call-done) | data formatting | bytes 8388608
  164.5 2.6 slice_bitcast_fusion.3
  167.1 2.2 pad_maximum_fusion
  169.4 5.0 %all-to-all-start = ((bf16[4,512,1024]{2,1,0:T(8,128)(2,1)}), bf16[4,512,1024]{2,1,0:T(8,128)(2,1)}, u32[]{:S(2)}, u32[]{:S(2)}) async-start(bf16[4,512,1024]{2,1,0:T(8,128)(2,1)} %pad_maximum_fusion), calls=%async_computation | async-start | bytes 8388608 | tf_op jit(solution)/shard_map/all_to_all | solution.py:83
  174.6 0.6 slice.50
  175.5 0.6 iota_compare_fusion.7
  176.3 0.9 select_reduce_fusion
  177.3 1.0 compare_and_fusion.2
  178.3 1.7 fusion.109
  180.1 87.4 %all-to-all-done = bf16[4,512,1024]{2,1,0:T(8,128)(2,1)} async-done(((bf16[4,512,1024]{2,1,0:T(8,128)(2,1)}), bf16[4,512,1024]{2,1,0:T(8,128)(2,1)}, u32[]{:S(2)}, u32[]{:S(2)}) %all-to-all-start) | async-done | bytes 4194336 | tf_op jit(solution)/shard_map/all_to_all | solution.py:83
  267.4 3.9 %fusion.108 = (bf16[1,512,1024]{2,1,0:T(8,128)(2,1)}, bf16[1,512,1024]{2,1,0:T(8,128)(2,1)S(1)}, bf16[1,512,1024]{2,1,0:T(8,128)(2,1)S(1)}, bf16[1,512,1024]{2,1,0:T(8,128)(2,1)S(1)}) fusion(bf16[4,512,1024]{2,1,0:T(8,128)(2,1)} %all-to-all-done), kind=kLoop, calls=%fused_computation.202 | loop fusion | bytes 8388608 | tf_op jit(solution)/shard_map/slice | solution.py:60
  271.3 2.3 copy.103
  273.6 1.3 copy.113
  275.4 0.5 copy.98
  276.0 1.6 fusion
  277.6 0.5 fusion.2
  278.1 0.6 copy-done
  282.5 0.7 fusion.19
  283.2 0.7 fusion.17
  283.8 0.7 fusion.15
  284.5 0.7 fusion.13
  285.4 0.9 copy.123
  (49 shorter events, 5.3 us)
Async XLA Ops:
  6.5 151.1 %all-gather.3.cloned.1.call-start = ((), (), s32[]{:S(2)}) async-start(), calls=%async_computation.1 | async-start | bytes 4227072 | tf_op jit(solution)/shard_map/all_gather | solution.py:81
  169.4 5.0 %copy-start.13 = (s32[4]{0:T(128)S(1)}, s32[4]{0:T(128)}, u32[]{:S(2)}) copy-start(s32[4]{0:T(128)} %param.10) | copy-start | bytes 52
  169.4 5.8 %copy-start.3 = (bf16[128,1024]{1,0:T(8,128)(2,1)S(1)}, bf16[128,1024]{1,0:T(8,128)(2,1)}, u32[]{:S(2)}) copy-start(bf16[128,1024]{1,0:T(8,128)(2,1)} %param.6) | copy-start | bytes 786436
  169.4 6.0 %copy-start.4 = (bf16[128,1024]{1,0:T(8,128)(2,1)S(1)}, bf16[128,1024]{1,0:T(8,128)(2,1)}, u32[]{:S(2)}) copy-start(bf16[128,1024]{1,0:T(8,128)(2,1)} %param.7) | copy-start | bytes 786436
  169.4 6.9 %copy-start.14 = (s32[4]{0:T(128)S(1)}, s32[4]{0:T(128)}, u32[]{:S(2)}) copy-start(s32[4]{0:T(128)} %param.11) | copy-start | bytes 52
  169.4 6.9 %copy-start.12 = (s32[512]{0:T(512)S(1)}, s32[512]{0:T(512)}, u32[]{:S(2)}) copy-start(s32[512]{0:T(512)} %param.9) | copy-start | bytes 6148
  169.4 98.0 %all-to-all-start = ((bf16[4,512,1024]{2,1,0:T(8,128)(2,1)}), bf16[4,512,1024]{2,1,0:T(8,128)(2,1)}, u32[]{:S(2)}, u32[]{:S(2)}) async-start(bf16[4,512,1024]{2,1,0:T(8,128)(2,1)} %pad_maximum_fusion), calls=%async_computation | async-start | bytes 8388608 | tf_op jit(solution)/shard_map/all_to_all | solution.py:83
  175.3 4.7 %copy-start.5 = (bf16[128,4,2,128]{3,2,1,0:T(2,128)(2,1)}, bf16[128,4,2,128]{3,2,1,0:T(2,128)(2,1)S(1)}, u32[]{:S(2)}) copy-start(bf16[128,4,2,128]{3,2,1,0:T(2,128)(2,1)S(1)} %reshape.518) | copy-start | bytes 786436
  176.1 3.9 %copy-start.9 = (pred[128]{0:T(512)(128)(4,1)}, pred[128]{0:T(512)(128)(4,1)S(1)}, u32[]{:S(2)}) copy-start(pred[128]{0:T(512)(128)(4,1)S(1)} %iota_compare_fusion.7) | copy-start | bytes 388
  276.0 1.6 copy-start.6
  277.6 1.2 copy-start
  278.1 1.3 copy-start.1
  278.1 1.3 copy-start.7
  279.3 0.7 copy-start.11
  279.3 0.9 copy-start.8
  279.4 1.3 copy-start.2
  281.4 1.1 copy-start.10
Sparse Core Ops, SparseCore 0:
  11.9 145.6 all-gather.2
